TPU v7x, 32 devices: a whole 2x2x4 slice. The times are simulated.
32 devices in a mesh: req: 16 (over z, x, core), kv: 2 (over y).
Axes of the slice: x: 2, y: 2, z: 4, core: 2. Of those that a mesh axis runs over, the one named last changes fastest.
Arguments:
- hidden: bfloat16 [32, 256, 1024], P('req', 'kv'), may hold values from -6 to 6
- queries: bfloat16 [32, 256, 1024], P('req', 'kv'), may hold values from -24 to 24
- span_kv: bfloat16 [32, 256, 8, 128], P('req', 'kv'), may hold values from -48 to 48
- cache: bfloat16 [32, 2048, 8, 128], P('req', 'kv'), may hold values from -48 to 48
- req_order: int32 [32], replicated, may hold values from 0 to 31, each once
- cached_len: int32 [32], replicated, may hold values from 8 to 2048, as said below
- out_weight: bfloat16 [1024, 1024], replicated, may hold values from -0.1875 to 0.1875
- norm_gain: float32 [1024], replicated, may hold values from 0.1 to 1.9
- expert_ids: int32 [8192, 8], P(('req', 'kv')), may hold values from 0 to 15, all different within a row; in each aligned block of 256 rows (0 to 255, 256 to 511, ...) at most 256 rows name the same one
- expert_weights: float32 [8192, 8], P(('req', 'kv')), may hold values from 0.05 to 0.5
- w_experts: bfloat16 [16, 3, 1024, 512], P('req', None, None, 'kv'), may hold values from -0.25 to 0.25
- block_map: int32 [32, 128], P('req'), may hold values from 0 to 4095, as said below
Outputs:
- layer_out: bfloat16 [32, 256, 1024], P('req', 'kv')
- decode_pool: bfloat16 [4096, 8, 16, 128], P('req', 'kv')
Inputs may be any that keep to these rules, and one draw needn't show every extreme that they name: `cached_len`: some request fills its cache. `block_map`: a permutation of the 4096 pool pages; pool page s belongs to req index s // 256; the pages that one kv index holds of the slots of one req index (positions of its cache share) go to every req index equally often. `expert_ids`: in the rows of one device no expert is named more than 256 times.
All inputs are finite; a program needn't handle non-finite values.
Results may differ from a plain program's by a relative error of at most 0.023.
Values may be sent and summed in bfloat16 or wider, within the bound.
No kernel may reach another device: no remote copies, remote signals or barrier semaphores. Data moves between devices by JAX's collectives and lax.ppermute only.
A program may use at most 128 MiB of HBM per device.

v0:
```python
import math
import jax
import jax.numpy as jnp
from jax import lax
from jax.sharding import PartitionSpec as P

BLOCK = 16


def lookup_lengths(req_order, cached_len, count):
    start = lax.axis_index("req") * count
    mine = lax.dynamic_slice_in_dim(req_order, start, count)
    match = mine[:, None] == jnp.arange(cached_len.shape[0], dtype=jnp.int32)[None, :]
    return jnp.sum(jnp.where(match, cached_len[None, :], 0), axis=1)


def score_block(query_rows, cache_rows, span_rows):
    span_count, group_count, width = query_rows.shape
    head_dim = cache_rows.shape[-1] // 2
    per_group = width // head_dim
    query_split = query_rows.reshape(span_count, group_count, per_group, head_dim)
    key_rows = jnp.concatenate([cache_rows[..., :head_dim], span_rows[..., :head_dim]], axis=0)
    value_rows = jnp.concatenate([cache_rows[..., head_dim:], span_rows[..., head_dim:]], axis=0)
    scores = jnp.einsum(
        "igsd,pgd->gsip", query_split, key_rows, preferred_element_type=jnp.float32
    ) * (1.0 / math.sqrt(head_dim))
    return (scores, value_rows)


def soft_weights(scores, allowed, value_rows):
    masked = jnp.where(allowed, scores, -1e30)
    row_max = jnp.max(masked, axis=-1, keepdims=True)
    probability = jnp.where(allowed, jnp.exp(masked - row_max), 0.0)
    prob_sum = jnp.sum(probability, axis=-1)
    weighted = jnp.einsum(
        "gsip,pgd->igsd",
        probability.astype(jnp.bfloat16),
        value_rows,
        preferred_element_type=jnp.float32,
    )
    return (weighted, jnp.transpose(row_max[..., 0], (2, 0, 1)), jnp.transpose(prob_sum, (2, 0, 1)))


def whole_request(operands):
    query_rows, cache_rows, span_rows, length = operands
    scores, value_rows = score_block(query_rows, cache_rows, span_rows)
    cached = cache_rows.shape[0]
    position = jnp.arange(scores.shape[-1])[None, :]
    query_pos = jnp.arange(query_rows.shape[0])[:, None]
    allowed = jnp.where(position < cached, position < length, position - cached <= query_pos)
    weighted, row_max, prob_sum = soft_weights(scores, allowed, value_rows)
    result = weighted / prob_sum[..., None]
    return result.reshape(query_rows.shape).astype(jnp.bfloat16)


def place_pages(page_rows, slot_numbers, slots_dev):
    owner_index = slot_numbers // slots_dev
    arrangement = jnp.argsort(owner_index, stable=True)
    return (page_rows[arrangement], (slot_numbers % slots_dev)[arrangement])


def body(
    hidden,
    queries,
    span_kv,
    cache,
    req_order,
    cached_len,
    out_weight,
    norm_gain,
    expert_ids,
    expert_weights,
    w_experts,
    block_map,
):
    local_reqs, local_tokens, width_model = hidden.shape
    row_count = local_reqs * local_tokens
    req_count = lax.axis_size("req")
    kv_count = lax.axis_size("kv")
    kv_heads = span_kv.shape[2]
    head_pair = span_kv.shape[3]
    group_width = queries.shape[2] // kv_heads
    group_count = kv_heads // kv_count
    slots_dev = local_reqs * block_map.shape[1]
    lengths = lookup_lengths(req_order, cached_len, local_reqs)
    queries_grouped = queries.reshape(local_reqs, local_tokens, kv_heads, group_width)
    cache_heads, span_heads, query_heads = (
        lax.all_to_all(cache, "kv", split_axis=2, concat_axis=1, tiled=True),
        lax.all_to_all(span_kv, "kv", split_axis=2, concat_axis=1, tiled=True),
        lax.all_to_all(queries_grouped, "kv", split_axis=2, concat_axis=1, tiled=True),
    )
    attn_heads = lax.map(whole_request, (query_heads, cache_heads, span_heads, lengths))
    attn = lax.all_to_all(attn_heads, "kv", split_axis=1, concat_axis=2, tiled=True).reshape(
        row_count, kv_heads * group_width
    )
    page_total = block_map.shape[1]
    visible = jnp.arange(cache_heads.shape[1])[None, :] < lengths[:, None]
    visible_cache = jnp.where(visible[:, :, None, None], cache_heads, jnp.zeros((), jnp.bfloat16))
    page_rows = (
        visible_cache.reshape(local_reqs, page_total, BLOCK, group_count, head_pair)
        .transpose(0, 1, 3, 2, 4)
        .reshape(local_reqs * page_total, group_count, BLOCK, head_pair)
    )
    sorted_pages, local_slot = place_pages(page_rows, block_map.reshape(-1), slots_dev)
    per_owner = sorted_pages.shape[0] // req_count
    outgoing = sorted_pages.reshape(req_count, per_owner, group_count, BLOCK, head_pair)
    arrived, where_to = (
        lax.all_to_all(outgoing, "req", split_axis=0, concat_axis=0, tiled=True),
        lax.all_to_all(
            local_slot.reshape(req_count, per_owner), "req", split_axis=0, concat_axis=0, tiled=True
        ),
    )
    decode_pool = (
        jnp.zeros((slots_dev, group_count, BLOCK, head_pair), jnp.bfloat16)
        .at[where_to.reshape(-1)]
        .set(arrived.reshape(-1, group_count, BLOCK, head_pair))
    )
    residual = hidden.reshape(row_count, width_model).astype(jnp.float32) + jnp.dot(
        attn, out_weight, preferred_element_type=jnp.float32
    )
    inverse_rms = lax.rsqrt(jnp.mean(residual * residual, axis=-1, keepdims=True) + 1e-05)
    normed = (residual * inverse_rms * norm_gain).astype(jnp.bfloat16)
    top_count = expert_ids.shape[1]
    exp_dev = w_experts.shape[0]
    experts = exp_dev * req_count
    capacity = min(row_count, 2 * row_count * top_count // experts)
    chosen = expert_ids.reshape(-1)
    onehot = (chosen[:, None] == jnp.arange(experts, dtype=jnp.int32)[None, :]).astype(jnp.int32)
    slot_rank = jnp.sum(onehot * (jnp.cumsum(onehot, axis=0) - 1), axis=1)
    target = chosen * capacity + slot_rank
    source_row = jnp.arange(chosen.shape[0]) // top_count
    buffer = (
        jnp.zeros((experts * capacity, width_model), jnp.bfloat16)
        .at[target]
        .set(normed[source_row])
        .reshape(experts, capacity, width_model)
    )
    full_weights = lax.all_gather(w_experts, "kv", axis=3, tiled=True)
    slot_block = lax.all_to_all(buffer, "req", split_axis=0, concat_axis=0, tiled=True)
    source_count = slot_block.shape[0] // exp_dev
    grouped = slot_block.reshape(source_count, exp_dev, slot_block.shape[1], width_model)
    gate_act = jnp.einsum(
        "sejd,edf->sejf", grouped, full_weights[:, 0], preferred_element_type=jnp.float32
    )
    up_act = jnp.einsum(
        "sejd,edf->sejf", grouped, full_weights[:, 1], preferred_element_type=jnp.float32
    )
    activated = (jax.nn.silu(gate_act) * up_act).astype(jnp.bfloat16)
    expert_out = jnp.einsum(
        "sejf,edf->sejd", activated, full_weights[:, 2], preferred_element_type=jnp.float32
    ).astype(jnp.bfloat16)
    returned = lax.all_to_all(
        expert_out.reshape(slot_block.shape), "req", split_axis=0, concat_axis=0, tiled=True
    )
    picked = returned.reshape(experts * capacity, width_model)[target].reshape(
        row_count, top_count, width_model
    )
    expert_sum = jnp.sum(expert_weights[..., None] * picked.astype(jnp.float32), axis=1)
    layer_out = (
        (residual + expert_sum).astype(jnp.bfloat16).reshape(local_reqs, local_tokens, width_model)
    )
    return (layer_out, decode_pool)


def solution(mesh):
    return jax.shard_map(
        body,
        mesh=mesh,
        in_specs=(
            P("req", "kv", None),
            P("req", "kv", None),
            P("req", "kv", None, None),
            P("req", "kv", None, None),
            P(),
            P(),
            P(),
            P(),
            P(("req", "kv"), None),
            P(("req", "kv"), None),
            P("req", None, None, "kv"),
            P("req", None),
        ),
        out_specs=(P("req", "kv", None), P("req", "kv", None, None)),
        check_vma=False,
    )
```

profile of v0, /device:TPU:11, one launch (start us, length us, event | category | flops | bytes accessed | tf_op | source)
XLA Modules:
  0.0 748.4 jit_solution(12969157909613193286)
XLA Ops:
  7.2 2.1 copy.81
  9.3 3.5 all-to-all-start.1
  12.8 1.3 copy.83
  14.1 0.8 copy.84
  14.9 5.2 all-to-all-done.1
  20.1 3.5 all-to-all-start.2
  24.0 5.0 copy.78
  29.0 1.0 all-to-all-done.2
  30.1 5.6 all-to-all-start
  35.7 4.5 reduce-window.6
  41.8 3.2 sort.17
  47.7 1.1 copy.82
  48.8 2.2 all_to_all.74
  51.0 1.0 copy.86
  52.0 28.7 %all-to-all-done = bf16[2,1024,8,128]{3,1,0,2:T(8,128)(2,1)} async-done(((bf16[2,1024,8,128]{3,1,0,2:T(8,128)(2,1)}), bf16[2,1024,8,128]{3,1,0,2:T(8,128)(2,1)}, u32[]{:S(2)}, u32[]{:S(2)}) %all-to-all-start) | async-done | bytes 4194336 | tf_op jit(solution)/shard_map/all_to_all | solution.py:88
  80.7 4.6 copy.80
  85.3 104.1 %while.12 = (s32[]{:T(128)}, bf16[2,256,4,128]{3,2,0,1:T(4,128)(2,1)}, bf16[2,2048,4,128]{3,1,2,0:T(8,128)(2,1)}, bf16[2,256,4,128]{1,3,2,0:T(8,128)(2,1)}, s32[...) while((s32[]{:T(128)}, bf16[2,256,4,128]{3,2,0,1:T(4,128)(2,1)}, ...), condition=%wide.region_4.5_spmd, body=%wide.region_1.4_spmd.sunk | while | flops 1251877888 | bytes 80653984 | solution.py:92
  85.3 3.0 constant_dynamic-slice_fusion.5
  88.3 4.0 copy.115
  92.3 2.8 fusion.64
  95.8 0.7 constant_dynamic-slice_fusion.4
  96.5 1.1 copy.114
  97.6 9.2 %fusion.65 = f32[4,2304,256,2]{2,1,3,0:T(8,128)} fusion(bf16[256,4,2,64]{0,3,2,1:T(8,128)(2,1)S(1)} %bitcast.190, bf16[256,4,64]{0,2,1:T(8,128)(2,1)} %get-tuple-element.183, bf16[2048,4,64]{0,2,1:T(8,128)(2,1)} %get-tuple-element.184), kind=kOutput, calls=%fused_computation.24.clone.1 | convolution fusion | flops 606339072 | bytes 20316160 | tf_op jit(solution)/shard_map/while/body/eval_jaxpr/igsd,pgd->gsip/dot_general | solution.py:24
  106.9 1.2 dynamic_slice.41
  108.7 2.7 fusion.66
  111.4 19.4 %fusion.67 = (f32[4,2,256]{2,1,0:T(2,128)S(1)}, bf16[4,2,256,2304]{2,3,1,0:T(8,128)(2,1)}) fusion(f32[4,2304,256,2]{2,1,3,0:T(8,128)} %fusion.65, pred[256,2304]{0,1:T(8,128)(4,1)} %fusion.66), kind=kOutput, calls=%fused_computation.99.clone.1 | output fusion | flops 37751040 | bytes 28909568 | tf_op jit(solution)/shard_map/while/body/eval_jaxpr/sub | solution.py:33
  130.9 5.5 fusion.68
  136.5 0.8 constant_dynamic-update-slice_fusion.2
  137.3 3.0 constant_dynamic-slice_fusion.5
  140.4 4.0 copy.115
  144.4 2.8 fusion.64
  147.9 0.7 constant_dynamic-slice_fusion.4
  148.6 1.1 copy.114
  149.7 9.2 %fusion.65 = f32[4,2304,256,2]{2,1,3,0:T(8,128)} fusion(bf16[256,4,2,64]{0,3,2,1:T(8,128)(2,1)S(1)} %bitcast.190, bf16[256,4,64]{0,2,1:T(8,128)(2,1)} %get-tuple-element.183, bf16[2048,4,64]{0,2,1:T(8,128)(2,1)} %get-tuple-element.184), kind=kOutput, calls=%fused_computation.24.clone.1 | convolution fusion | flops 606339072 | bytes 20316160 | tf_op jit(solution)/shard_map/while/body/eval_jaxpr/igsd,pgd->gsip/dot_general | solution.py:24
  158.9 1.2 dynamic_slice.41
  160.8 2.7 fusion.66
  163.5 19.4 %fusion.67 = (f32[4,2,256]{2,1,0:T(2,128)S(1)}, bf16[4,2,256,2304]{2,3,1,0:T(8,128)(2,1)}) fusion(f32[4,2304,256,2]{2,1,3,0:T(8,128)} %fusion.65, pred[256,2304]{0,1:T(8,128)(4,1)} %fusion.66), kind=kOutput, calls=%fused_computation.99.clone.1 | output fusion | flops 37751040 | bytes 28909568 | tf_op jit(solution)/shard_map/while/body/eval_jaxpr/sub | solution.py:33
  182.9 5.5 fusion.68
  188.6 0.8 constant_dynamic-update-slice_fusion.2
  189.4 3.6 all-to-all-start.3
  193.1 1.9 gather_fusion.1
  196.4 2.0 all-to-all-done.3
  198.4 10.7 %all-to-all-start.6 = ((s32[16,1,16]{2,1,0:T(1,128)}), s32[16,1,16]{2,1,0:T(1,128)S(1)}, u32[]{:S(2)}, u32[]{:S(2)}) async-start(s32[16,1,16]{2,1,0:T(1,128)} %all_to_all.84), calls=%async_computation.6 | async-start | bytes 16384 | tf_op jit(solution)/shard_map/all_to_all | solution.py:109
  209.3 1.2 reshape.267
  210.5 2.0 multiply_reduce_fusion
  212.5 0.9 multiply_convert_fusion
  213.5 33.0 %scatter_custom_fusion = bf16[4096,1024]{1,0:T(8,128)(2,1)} fusion(s32[2048]{0:T(1024)S(1)} %bitcast.205, bf16[256,1024]{1,0:T(8,128)(2,1)} %multiply_convert_fusion, s32[2048]{0:T(1024)S(1)} %broadcast_clamp_fusion.1, bf16[]{:T(256)} %constant.114.clone.1), kind=kCustom, calls=%fused_computation.49 | custom fusion | bytes 8389120 | tf_op jit(solution)/shard_map/scatter | solution.py:135
  246.4 6.4 all-to-all-start.4
  253.5 2.6 select_bitcast_fusion
  256.1 3.3 copy.96
  259.4 5.2 gather_fusion.2
  264.6 170.4 %all-to-all-done.4 = bf16[16,256,1024]{2,1,0:T(8,128)(2,1)} async-done(((bf16[16,256,1024]{2,1,0:T(8,128)(2,1)}), bf16[16,256,1024]{2,1,0:T(8,128)(2,1)}, u32[]{:S(2)}, u32[]{:S(2)}) %all-to-all-start.4) | async-done | bytes 8388640 | tf_op jit(solution)/shard_map/all_to_all | solution.py:139
  435.0 4.9 all-to-all-start.7
  440.6 46.2 %all-gather.2.cloned.1.call-done = bf16[1,3,1024,512]{3,2,1,0:T(8,128)(2,1)} async-done(((bf16[1,3,1024,256]{3,2,1,0:T(8,128)(2,1)}), bf16[1,3,1024,512]{3,2,1,0:T(8,128)(2,1)}) %all-gather.2.cloned.1.call-update) | async-done | bytes 3145744 | tf_op jit(solution)/shard_map/all_gather | solution.py:138
  486.8 11.4 %fusion.38 = f32[16,256,512]{2,1,0:T(8,128)} fusion(bf16[16,256,1024]{2,1,0:T(8,128)(2,1)} %all-to-all-done.4, bf16[1,3,1024,512]{3,2,1,0:T(8,128)(2,1)} %all-gather.2.cloned.1.call-done), kind=kOutput, calls=%fused_computation.58 | convolution fusion | flops 4294967296 | bytes 17825792 | tf_op jit(solution)/shard_map/sejd,edf->sejf/dot_general | solution.py:142
  498.2 16.0 %convolution_convert_fusion = bf16[16,256,1024]{2,1,0:T(8,128)(2,1)} fusion(f32[16,256,512]{2,1,0:T(8,128)} %fusion.38, bf16[16,256,1024]{2,1,0:T(8,128)(2,1)} %all-to-all-done.4, bf16[1,3,1024,512]{3,2,1,0:T(8,128)(2,1)} %all-gather.2.cloned.1.call-done), kind=kOutput, calls=%fused_computation.47 | convolution fusion | flops 8606711808 | bytes 27262976 | tf_op jit(solution)/shard_map/sejf,edf->sejd/dot_general | solution.py:149
  514.2 18.2 %all-to-all-done.7 = bf16[16,16,4,16,128]{4,3,2,1,0:T(8,128)(2,1)} async-done(((bf16[16,16,4,16,128]{4,3,2,1,0:T(8,128)(2,1)}), bf16[16,16,4,16,128]{4,3,2,1,0:T(8,128)(2,1)}, u32[]{:S(2)}, u32[]{:S(2)}) %all-to-all-start.7) | async-done | bytes 4194336 | tf_op jit(solution)/shard_map/all_to_all | solution.py:108
  532.4 5.3 all-to-all-start.5
  539.1 3.1 broadcast_in_dim.106
  542.2 33.5 %scatter_fusion = bf16[256,4,16,128]{3,2,1,0:T(8,128)(2,1)} fusion(bf16[256,4,16,128]{3,2,1,0:T(8,128)(2,1)} %broadcast_in_dim.106, s32[256]{0:T(256)S(1)} %bitcast.209, bf16[256,4,16,128]{3,2,1,0:T(8,128)(2,1)} %bitcast.57), kind=kCustom, calls=%fused_computation.5 | custom fusion | bytes 12583936 | tf_op jit(solution)/shard_map/scatter | solution.py:116
  575.7 144.2 %all-to-all-done.5 = bf16[16,256,1024]{2,1,0:T(8,128)(2,1)} async-done(((bf16[16,256,1024]{2,1,0:T(8,128)(2,1)}), bf16[16,256,1024]{2,1,0:T(8,128)(2,1)}, u32[]{:S(2)}, u32[]{:S(2)}) %all-to-all-start.5) | async-done | bytes 8388640 | tf_op jit(solution)/shard_map/all_to_all | solution.py:152
  719.9 15.5 %gather_fusion = bf16[2048,1024]{1,0:T(8,128)(2,1)} fusion(bf16[4096,1024]{1,0:T(8,128)(2,1)} %bitcast.46, s32[2048]{0:T(1024)S(1)} %broadcast_clamp_fusion), kind=kCustom, calls=%fused_computation.1 | custom fusion | bytes 8396800 | tf_op jit(solution)/shard_map/gather | solution.py:155
  735.3 4.8 fusion.26
  740.1 1.0 add_convert_fusion
  (73 shorter events, 12.0 us)
Async XLA Ops:
  7.2 203.3 %copy-start = (bf16[1024,1024]{1,0:T(8,128)(2,1)S(1)}, bf16[1024,1024]{1,0:T(8,128)(2,1)}, u32[]{:S(2)}) copy-start(bf16[1024,1024]{1,0:T(8,128)(2,1)} %param.20) | copy-start | bytes 6291460
  7.2 16.5 %copy-start.4 = (s32[256,8]{0,1:T(8,128)S(1)}, s32[256,8]{0,1:T(8,128)}, u32[]{:S(2)}) copy-start(s32[256,8]{0,1:T(8,128)} %param.22) | copy-start | bytes 24580
  9.3 10.9 %all-to-all-start.1 = ((bf16[2,128,8,128]{3,1,0,2:T(8,128)(2,1)}), bf16[2,128,8,128]{3,1,0,2:T(8,128)(2,1)S(1)}, u32[]{:S(2)}, u32[]{:S(2)}) async-start(bf16[2,128,8,128]{3,1,0,2:T(8,128)(2,1)} %copy.81), calls=%async_computation.1 | async-start | bytes 1048576 | tf_op jit(solution)/shard_map/all_to_all | solution.py:89
  20.1 9.9 %all-to-all-start.2 = ((bf16[2,128,8,128]{1,3,0,2:T(8,128)(2,1)}), bf16[2,128,8,128]{1,3,0,2:T(8,128)(2,1)S(1)}, u32[]{:S(2)}, u32[]{:S(2)}) async-start(bf16[2,128,8,128]{1,3,0,2:T(8,128)(2,1)} %copy.84), calls=%async_computation.2 | async-start | bytes 1048576 | tf_op jit(solution)/shard_map/all_to_all | solution.py:90
  29.0 12.1 %copy-start.10 = (s32[32]{0:T(128)S(1)}, s32[32]{0:T(128)}, u32[]{:S(2)}) copy-start(s32[32]{0:T(128)} %param.18) | copy-start | bytes 388
  29.0 12.2 %copy-start.9 = (s32[2,128]{1,0:T(2,128)S(1)}, s32[2,128]{1,0:T(2,128)}, u32[]{:S(2)}) copy-start(s32[2,128]{1,0:T(2,128)} %param.25) | copy-start | bytes 3076
  29.0 16.0 %copy-start.11 = (s32[32]{0:T(128)S(1)}, s32[32]{0:T(128)}, u32[]{:S(2)}) copy-start(s32[32]{0:T(128)} %param.19) | copy-start | bytes 388
  30.1 50.6 %all-to-all-start = ((bf16[2,1024,8,128]{3,1,0,2:T(8,128)(2,1)}), bf16[2,1024,8,128]{3,1,0,2:T(8,128)(2,1)}, u32[]{:S(2)}, u32[]{:S(2)}) async-start(bf16[2,1024,8,128]{3,1,0,2:T(8,128)(2,1)} %copy.78), calls=%async_computation | async-start | bytes 8388608 | tf_op jit(solution)/shard_map/all_to_all | solution.py:88
  85.3 107.8 %copy-start.8 = (s32[256]{0:T(256)S(1)}, s32[256]{0:T(256)}, u32[]{:S(2)}) copy-start(s32[256]{0:T(256)} %compare_select_fusion.3) | copy-start | bytes 3076
  85.3 107.8 %copy-start.1 = (s32[256]{0:T(256)S(1)}, s32[256]{0:T(256)}, u32[]{:S(2)}) copy-start(s32[256]{0:T(256)} %get-tuple-element.133) | copy-start | bytes 3076
  92.3 2.8 copy-start.2
  92.3 3.5 copy-start.3
  144.4 2.8 copy-start.2
  144.4 3.5 copy-start.3
  189.4 23.1 %copy-start.7 = (f32[1024]{0:T(1024)S(1)}, f32[1024]{0:T(1024)}, u32[]{:S(2)}) copy-start(f32[1024]{0:T(1024)} %param.21) | copy-start | bytes 12292
  189.4 9.0 %all-to-all-start.3 = ((bf16[2,256,4,128]{3,2,0,1:T(4,128)(2,1)}), bf16[2,256,4,128]{3,2,0,1:T(4,128)(2,1)S(1)}, u32[]{:S(2)}, u32[]{:S(2)}) async-start(bf16[2,256,4,128]{3,2,0,1:T(4,128)(2,1)} %get-tuple-element.80), calls=%async_computation.3 | async-start | bytes 1048576 | tf_op jit(solution)/shard_map/all_to_all | solution.py:93
  195.0 18.4 %copy-start.5 = (s32[2048,1]{0,1:T(1,128)S(1)}, s32[2048,1]{0,1:T(1,128)}, u32[]{:S(2)}) copy-start(s32[2048,1]{0,1:T(1,128)} %compare_select_fusion.1) | copy-start | bytes 24580
  198.4 48.0 %all-to-all-start.6 = ((s32[16,1,16]{2,1,0:T(1,128)}), s32[16,1,16]{2,1,0:T(1,128)S(1)}, u32[]{:S(2)}, u32[]{:S(2)}) async-start(s32[16,1,16]{2,1,0:T(1,128)} %all_to_all.84), calls=%async_computation.6 | async-start | bytes 16384 | tf_op jit(solution)/shard_map/all_to_all | solution.py:109
  246.4 188.6 %all-to-all-start.4 = ((bf16[16,256,1024]{2,1,0:T(8,128)(2,1)}), bf16[16,256,1024]{2,1,0:T(8,128)(2,1)}, u32[]{:S(2)}, u32[]{:S(2)}) async-start(bf16[16,256,1024]{2,1,0:T(8,128)(2,1)} %bitcast.189), calls=%async_computation.4 | async-start | bytes 16777216 | tf_op jit(solution)/shard_map/all_to_all | solution.py:139
  435.0 97.4 %all-to-all-start.7 = ((bf16[16,16,4,16,128]{4,3,2,1,0:T(8,128)(2,1)}), bf16[16,16,4,16,128]{4,3,2,1,0:T(8,128)(2,1)}, u32[]{:S(2)}, u32[]{:S(2)}) async-start(bf16[16,16,4,16,128]{4,3,2,1,0:T(8,128)(2,1)} %bitcast.192), calls=%async_computation.7 | async-start | bytes 8388608 | tf_op jit(solution)/shard_map/all_to_all | solution.py:108
  439.9 46.9 %all-gather.2.cloned.1.call-start = ((), (), s32[]{:S(2)}) async-start(), calls=%async_computation.8 | async-start | bytes 4718592 | tf_op jit(solution)/shard_map/all_gather | solution.py:138
  514.2 23.5 %copy-start.6 = (f32[256,8]{0,1:T(8,128)S(1)}, f32[256,8]{0,1:T(8,128)}, u32[]{:S(2)}) copy-start(f32[256,8]{0,1:T(8,128)} %param.23) | copy-start | bytes 24580
  532.4 187.5 %all-to-all-start.5 = ((bf16[16,256,1024]{2,1,0:T(8,128)(2,1)}), bf16[16,256,1024]{2,1,0:T(8,128)(2,1)}, u32[]{:S(2)}, u32[]{:S(2)}) async-start(bf16[16,256,1024]{2,1,0:T(8,128)(2,1)} %convolution_convert_fusion), calls=%async_computation.5 | async-start | bytes 16777216 | tf_op jit(solution)/shard_map/all_to_all | solution.py:152
Sparse Core Ops, SparseCore 0:
  442.3 44.5 all-gather.1
where the time goes:
time: 760 us; the launch traced here: 748 us
  waiting for transfers between devices  417 us (55%)
  local copies, waits for them, and re-layouts  147 us (19%)
  other arithmetic  68.1 us (9%)
  matrix products  58.8 us (8%)
  starting transfers between devices  43.5 us (6%)
  between operations  14.8 us (2%)
    all_to_all x1, waiting for transfers between devices, body(): lax.all_to_all(buffer, 'req', split_axis=0, concat_axis=0, tiled=True)  170 us
    all_to_all x1, waiting for transfers between devices, body(): lax.all_to_all(expert_out.reshape(slot_block.shape), 'req', split_axis=0,...  144 us
    all_gather x1, waiting for transfers between devices, body(): full_weights = lax.all_gather(w_experts, 'kv', axis=3, tiled=True)  46.2 us
    sub x2, other arithmetic, soft_weights(): probability = jnp.where(allowed, jnp.exp(masked - row_max), 0.0)  38.9 us
    scatter x1, local copies, waits for them, and re-layouts, body(): decode_pool = jnp.zeros((slots_dev, group_count, BLOCK, head_pair), jnp.b...  33.5 us
    scatter x1, local copies, waits for them, and re-layouts, body(): buffer = jnp.zeros((experts * capacity, width_model), jnp.bfloat16).at[ta...  33 us
    all_to_all x1, waiting for transfers between devices, body(): lax.all_to_all(cache, 'kv', split_axis=2, concat_axis=1, tiled=True)  28.7 us
    dynamic_slice x10, local copies, waits for them, and re-layouts, body(): lax.map(whole_request, (query_heads, cache_heads, span_heads, lengths))  20.2 us
  transfers between devices with their start and end apart: 9, of which 8 were waited for; matrix products, arithmetic and copies ran while one was open for 19% of the time, Pallas kernels for 0%

commit v1 on v0

--- a/solution.py
+++ b/solution.py
@@ -5,6 +5,22 @@
 from jax.sharding import PartitionSpec as P
 
 BLOCK = 16
+
+
+def swapped_with_each(x, axis, split, join):
+    ways, here = (lax.axis_size(axis), lax.axis_index(axis))
+    width = x.shape[split] // ways
+    shape = list(x.shape)
+    shape[split] = width
+    height = shape[join]
+    shape[join] = height * ways
+    full = jnp.zeros(shape, x.dtype)
+    for mask in range(ways):
+        part = lax.dynamic_slice_in_dim(x, (here ^ mask) * width, width, axis=split)
+        if mask:
+            part = lax.ppermute(part, axis, [(d, d ^ mask) for d in range(ways)])
+        full = lax.dynamic_update_slice_in_dim(full, part, (here ^ mask) * height, axis=join)
+    return full
 
 
 def lookup_lengths(req_order, cached_len, count):
@@ -105,7 +121,7 @@
     per_owner = sorted_pages.shape[0] // req_count
     outgoing = sorted_pages.reshape(req_count, per_owner, group_count, BLOCK, head_pair)
     arrived, where_to = (
-        lax.all_to_all(outgoing, "req", split_axis=0, concat_axis=0, tiled=True),
+        swapped_with_each(outgoing, "req", 0, 0),
         lax.all_to_all(
             local_slot.reshape(req_count, per_owner), "req", split_axis=0, concat_axis=0, tiled=True
         ),

time: 760 us -> 817 us (1.075)
  starting transfers between devices: 43.5 us -> 70.9 us
  local copies, waits for them, and re-layouts: 147 us -> 165 us
  waiting for transfers between devices: 417 us -> 427 us
    ppermute x0 -> x15, waiting for transfers between devices: none -> 207 us  [swapped_with_each(): part = lax.ppermute(part, axis, [(d, d ^ mask) for d in range(ways)])]
    all_to_all x1, waiting for transfers between devices: 144 us -> 0.01 us  [body(): lax.all_to_all(expert_out.reshape(slot_block.shape), 'req', split_axis=0,...]
    all_gather x1, waiting for transfers between devices: 46.2 us -> 0.01 us  [body(): full_weights = lax.all_gather(w_experts, 'kv', axis=3, tiled=True)]
    ppermute x0 -> x15, starting transfers between devices: none -> 32.2 us  [swapped_with_each(): part = lax.ppermute(part, axis, [(d, d ^ mask) for d in range(ways)])]
    all_to_all x1 -> x0, waiting for transfers between devices: 18.2 us -> none  [body(): lax.all_to_all(outgoing, 'req', split_axis=0, concat_axis=0, tiled=True)]
    dynamic_update_slice x0 -> x15, local copies, waits for them, and re-layouts: none -> 11.8 us  [swapped_with_each(): lax.dynamic_update_slice_in_dim(full, part, (here ^ mask) * height, axis=...]
  transfers between devices with their start and end apart: 9 -> 23, of which waited for: 8 -> 18; matrix products, arithmetic and copies ran while one was open for 19% -> 15% of each run, Pallas kernels for 0% -> 0%
where the time goes in v1:
time: 817 us; the launch traced here: 802 us
  waiting for transfers between devices  427 us (52%)
  local copies, waits for them, and re-layouts  165 us (20%)
  starting transfers between devices  70.9 us (9%)
  other arithmetic  67.5 us (8%)
  matrix products  56.2 us (7%)
  between operations  14.6 us (2%)
    ppermute x15, waiting for transfers between devices, swapped_with_each(): part = lax.ppermute(part, axis, [(d, d ^ mask) for d in range(ways)])  207 us
    all_to_all x1, waiting for transfers between devices, body(): lax.all_to_all(buffer, 'req', split_axis=0, concat_axis=0, tiled=True)  176 us
    sub x2, other arithmetic, soft_weights(): probability = jnp.where(allowed, jnp.exp(masked - row_max), 0.0)  38.7 us
    scatter x1, local copies, waits for them, and re-layouts, body(): decode_pool = jnp.zeros((slots_dev, group_count, BLOCK, head_pair), jnp.b...  33.5 us
    scatter x1, local copies, waits for them, and re-layouts, body(): buffer = jnp.zeros((experts * capacity, width_model), jnp.bfloat16).at[ta...  33.3 us
    all_to_all x1, waiting for transfers between devices, body(): lax.all_to_all(cache, 'kv', split_axis=2, concat_axis=1, tiled=True)  32.6 us
    ppermute x15, starting transfers between devices, swapped_with_each(): part = lax.ppermute(part, axis, [(d, d ^ mask) for d in range(ways)])  32.2 us
    dynamic_slice x10, local copies, waits for them, and re-layouts, body(): lax.map(whole_request, (query_heads, cache_heads, span_heads, lengths))  18.9 us
  transfers between devices with their start and end apart: 23, of which 18 were waited for; matrix products, arithmetic and copies ran while one was open for 15% of the time, Pallas kernels for 0%

profile of v1, /device:TPU:11, one launch (start us, length us, event | category | flops | bytes accessed | tf_op | source)
XLA Modules:
  0.0 802.1 jit_solution(10293400919820019693)
XLA Ops:
  7.2 2.1 copy.81
  9.3 3.5 all-to-all-start.1
  14.9 5.2 all-to-all-done.1
  20.1 3.5 all-to-all-start.2
  23.6 5.0 copy.78
  30.1 5.6 all-to-all-start
  36.9 4.5 reduce-window.6
  44.8 2.2 all_to_all.71
  48.0 32.6 %all-to-all-done = bf16[2,1024,8,128]{3,1,0,2:T(8,128)(2,1)} async-done(((bf16[2,1024,8,128]{3,1,0,2:T(8,128)(2,1)}), bf16[2,1024,8,128]{3,1,0,2:T(8,128)(2,1)}, u32[]{:S(2)}, u32[]{:S(2)}) %all-to-all-start) | async-done | bytes 4194336 | tf_op jit(solution)/shard_map/all_to_all | solution.py:104
  80.6 4.6 copy.80
  85.2 99.9 %while.12 = (s32[]{:T(128)}, bf16[2,256,4,128]{3,2,0,1:T(4,128)(2,1)}, bf16[2,2048,4,128]{3,1,2,0:T(8,128)(2,1)}, bf16[2,256,4,128]{1,3,2,0:T(8,128)(2,1)}, s32[...) while((s32[]{:T(128)}, bf16[2,256,4,128]{3,2,0,1:T(4,128)(2,1)}, ...), condition=%wide.region_4.5_spmd, body=%wide.region_1.4_spmd.sunk | while | flops 1251877888 | bytes 76983440 | solution.py:108
  88.0 3.1 constant_dynamic-slice_fusion.20
  91.1 4.0 copy.115
  96.8 7.9 fusion.65
  106.7 2.7 fusion.66
  109.4 19.4 %fusion.67 = (f32[4,2,256]{2,1,0:T(2,128)S(1)}, bf16[4,2,256,2304]{2,3,1,0:T(8,128)(2,1)}) fusion(f32[4,2304,256,2]{2,1,3,0:T(8,128)} %fusion.65, pred[256,2304]{0,1:T(8,128)(4,1)} %fusion.66), kind=kOutput, calls=%fused_computation.130.clone.1 | output fusion | flops 37751040 | bytes 28909568 | tf_op jit(solution)/shard_map/while/body/eval_jaxpr/sub | solution.py:49
  128.8 5.4 fusion.68
  138.0 3.1 constant_dynamic-slice_fusion.20
  141.0 4.0 copy.115
  146.8 7.9 fusion.65
  156.7 2.7 fusion.66
  159.4 19.4 %fusion.67 = (f32[4,2,256]{2,1,0:T(2,128)S(1)}, bf16[4,2,256,2304]{2,3,1,0:T(8,128)(2,1)}) fusion(f32[4,2304,256,2]{2,1,3,0:T(8,128)} %fusion.65, pred[256,2304]{0,1:T(8,128)(4,1)} %fusion.66), kind=kOutput, calls=%fused_computation.130.clone.1 | output fusion | flops 37751040 | bytes 28909568 | tf_op jit(solution)/shard_map/while/body/eval_jaxpr/sub | solution.py:49
  178.7 5.4 fusion.68
  185.2 4.1 all-to-all-start.3
  190.0 4.7 all-to-all-done.3
  196.0 2.0 multiply_reduce_fusion
  199.0 33.3 %scatter_custom_fusion = bf16[4096,1024]{1,0:T(8,128)(2,1)} fusion(s32[2048]{0:T(1024)S(1)} %bitcast.205, bf16[256,1024]{1,0:T(8,128)(2,1)} %multiply_convert_fusion, s32[2048]{0:T(1024)S(1)} %broadcast_clamp_fusion.1, bf16[]{:T(256)} %constant.129.clone.1), kind=kCustom, calls=%fused_computation.49 | custom fusion | bytes 8389120 | tf_op jit(solution)/shard_map/scatter | solution.py:151
  232.3 10.6 %all-to-all-start.4 = ((bf16[16,256,1024]{2,1,0:T(8,128)(2,1)}), bf16[16,256,1024]{2,1,0:T(8,128)(2,1)}, u32[]{:S(2)}, u32[]{:S(2)}) async-start(bf16[16,256,1024]{2,1,0:T(8,128)(2,1)} %bitcast.189), calls=%async_computation.4 | async-start | bytes 16777216 | tf_op jit(solution)/shard_map/all_to_all | solution.py:155
  243.7 3.2 sort.17
  246.8 1.9 gather_fusion.1
  249.5 175.8 %all-to-all-done.4 = bf16[16,256,1024]{2,1,0:T(8,128)(2,1)} async-done(((bf16[16,256,1024]{2,1,0:T(8,128)(2,1)}), bf16[16,256,1024]{2,1,0:T(8,128)(2,1)}, u32[]{:S(2)}, u32[]{:S(2)}) %all-to-all-start.4) | async-done | bytes 8388640 | tf_op jit(solution)/shard_map/all_to_all | solution.py:155
  425.2 4.9 all-to-all-start.6
  430.2 11.4 %fusion.38 = f32[16,256,512]{2,1,0:T(8,128)} fusion(bf16[16,256,1024]{2,1,0:T(8,128)(2,1)} %all-to-all-done.4, bf16[1,3,1024,512]{3,2,1,0:T(8,128)(2,1)} %all-gather.2.cloned.1.call-done), kind=kOutput, calls=%fused_computation.58 | convolution fusion | flops 4294967296 | bytes 17825792 | tf_op jit(solution)/shard_map/sejd,edf->sejf/dot_general | solution.py:158
  441.5 16.0 %convolution_convert_fusion = bf16[16,256,1024]{2,1,0:T(8,128)(2,1)} fusion(f32[16,256,512]{2,1,0:T(8,128)} %fusion.38, bf16[16,256,1024]{2,1,0:T(8,128)(2,1)} %all-to-all-done.4, bf16[1,3,1024,512]{3,2,1,0:T(8,128)(2,1)} %all-gather.2.cloned.1.call-done), kind=kOutput, calls=%fused_computation.47 | convolution fusion | flops 8606711808 | bytes 27262976 | tf_op jit(solution)/shard_map/sejf,edf->sejd/dot_general | solution.py:165
  458.2 6.4 all-to-all-start.5
  465.4 2.6 select_bitcast_fusion
  468.0 3.3 copy.96
  471.3 5.2 gather_fusion.2
  476.5 3.0 broadcast_in_dim.111
  479.6 2.4 constant_dynamic-slice_fusion.2
  483.7 1.9 reduce.5
  491.6 24.6 %collective-permute-done.1 = bf16[1,16,4,16,128]{4,3,2,1,0:T(8,128)(2,1)S(1)} collective-permute-done((bf16[1,16,4,16,128]{4,3,2,1,0:T(8,128)(2,1)}, bf16[1,16,4,16,128]{4,3,2,1,0:T(8,128)(2,1)S(1)}, u32[]{:S(2)}, u32[]{:S(2)}) %collective-permute-start.1) | collective-permute-done | bytes 262176 | tf_op jit(solution)/shard_map/ppermute | solution.py:21
  516.3 3.4 collective-permute-start.6
  522.1 2.2 collective-permute-start.7
  524.9 82.3 %collective-permute-done.3 = bf16[1,16,4,16,128]{4,3,2,1,0:T(8,128)(2,1)S(1)} collective-permute-done((bf16[1,16,4,16,128]{4,3,2,1,0:T(8,128)(2,1)}, bf16[1,16,4,16,128]{4,3,2,1,0:T(8,128)(2,1)S(1)}, u32[]{:S(2)}, u32[]{:S(2)}) %collective-permute-start.3) | collective-permute-done | bytes 262176 | tf_op jit(solution)/shard_map/ppermute | solution.py:21
  609.5 4.3 collective-permute-done.4
  614.5 3.1 collective-permute-done.5
  617.6 7.3 collective-permute-start.10
  625.6 6.2 collective-permute-start.11
  632.6 45.7 %collective-permute-done.7 = bf16[1,16,4,16,128]{4,3,2,1,0:T(8,128)(2,1)S(1)} collective-permute-done((bf16[1,16,4,16,128]{4,3,2,1,0:T(8,128)(2,1)}, bf16[1,16,4,16,128]{4,3,2,1,0:T(8,128)(2,1)S(1)}, u32[]{:S(2)}, u32[]{:S(2)}) %collective-permute-start.7) | collective-permute-done | bytes 262176 | tf_op jit(solution)/shard_map/ppermute | solution.py:21
  678.2 2.5 collective-permute-start.12
  681.5 2.2 collective-permute-done.8
  683.7 2.5 collective-permute-start.13
  687.0 8.1 %collective-permute-done.9 = bf16[1,16,4,16,128]{4,3,2,1,0:T(8,128)(2,1)S(1)} collective-permute-done((bf16[1,16,4,16,128]{4,3,2,1,0:T(8,128)(2,1)}, bf16[1,16,4,16,128]{4,3,2,1,0:T(8,128)(2,1)S(1)}, u32[]{:S(2)}, u32[]{:S(2)}) %collective-permute-start.9) | collective-permute-done | bytes 262176 | tf_op jit(solution)/shard_map/ppermute | solution.py:21
  695.1 2.5 collective-permute-start.14
  698.3 13.6 %collective-permute-done.10 = bf16[1,16,4,16,128]{4,3,2,1,0:T(8,128)(2,1)S(1)} collective-permute-done((bf16[1,16,4,16,128]{4,3,2,1,0:T(8,128)(2,1)}, bf16[1,16,4,16,128]{4,3,2,1,0:T(8,128)(2,1)S(1)}, u32[]{:S(2)}, u32[]{:S(2)}) %collective-permute-start.10) | collective-permute-done | bytes 262176 | tf_op jit(solution)/shard_map/ppermute | solution.py:21
  712.7 6.9 collective-permute-done.11
  720.2 5.8 collective-permute-done.12
  726.8 3.9 collective-permute-done.13
  731.5 5.1 collective-permute-done.14
  737.2 3.1 broadcast_in_dim.109
  740.3 33.5 %scatter_fusion = bf16[256,4,16,128]{3,2,1,0:T(8,128)(2,1)} fusion(bf16[256,4,16,128]{3,2,1,0:T(8,128)(2,1)} %broadcast_in_dim.109, s32[256]{0:T(256)S(1)} %bitcast.208, bf16[256,4,16,128]{3,2,1,0:T(8,128)(2,1)} %bitcast.57), kind=kCustom, calls=%fused_computation.5 | custom fusion | bytes 12583936 | tf_op jit(solution)/shard_map/scatter | solution.py:132
  773.8 15.4 %gather_fusion = bf16[2048,1024]{1,0:T(8,128)(2,1)} fusion(bf16[4096,1024]{1,0:T(8,128)(2,1)} %bitcast.46, s32[2048]{0:T(1024)S(1)} %broadcast_clamp_fusion), kind=kCustom, calls=%fused_computation.1 | custom fusion | bytes 8396800 | tf_op jit(solution)/shard_map/gather | solution.py:171
  789.2 4.8 fusion.26
  (113 shorter events, 51.8 us)
Async XLA Ops:
  7.2 188.9 %copy-start = (bf16[1024,1024]{1,0:T(8,128)(2,1)S(1)}, bf16[1024,1024]{1,0:T(8,128)(2,1)}, u32[]{:S(2)}) copy-start(bf16[1024,1024]{1,0:T(8,128)(2,1)} %param.20) | copy-start | bytes 6291460
  9.3 10.9 %all-to-all-start.1 = ((bf16[2,128,8,128]{3,1,0,2:T(8,128)(2,1)}), bf16[2,128,8,128]{3,1,0,2:T(8,128)(2,1)S(1)}, u32[]{:S(2)}, u32[]{:S(2)}) async-start(bf16[2,128,8,128]{3,1,0,2:T(8,128)(2,1)} %copy.81), calls=%async_computation.1 | async-start | bytes 1048576 | tf_op jit(solution)/shard_map/all_to_all | solution.py:105
  20.1 9.9 %all-to-all-start.2 = ((bf16[2,128,8,128]{1,3,0,2:T(8,128)(2,1)}), bf16[2,128,8,128]{1,3,0,2:T(8,128)(2,1)S(1)}, u32[]{:S(2)}, u32[]{:S(2)}) async-start(bf16[2,128,8,128]{1,3,0,2:T(8,128)(2,1)} %copy.84), calls=%async_computation.2 | async-start | bytes 1048576 | tf_op jit(solution)/shard_map/all_to_all | solution.py:106
  28.6 7.1 copy-start.4
  28.6 13.4 %copy-start.9 = (s32[32]{0:T(128)S(1)}, s32[32]{0:T(128)}, u32[]{:S(2)}) copy-start(s32[32]{0:T(128)} %param.18) | copy-start | bytes 388
  28.6 13.5 %copy-start.10 = (s32[32]{0:T(128)S(1)}, s32[32]{0:T(128)}, u32[]{:S(2)}) copy-start(s32[32]{0:T(128)} %param.19) | copy-start | bytes 388
  30.1 50.6 %all-to-all-start = ((bf16[2,1024,8,128]{3,1,0,2:T(8,128)(2,1)}), bf16[2,1024,8,128]{3,1,0,2:T(8,128)(2,1)}, u32[]{:S(2)}, u32[]{:S(2)}) async-start(bf16[2,1024,8,128]{3,1,0,2:T(8,128)(2,1)} %copy.78), calls=%async_computation | async-start | bytes 8388608 | tf_op jit(solution)/shard_map/all_to_all | solution.py:104
  85.2 104.0 %copy-start.6 = (s32[2048,1]{0,1:T(1,128)S(1)}, s32[2048,1]{0,1:T(1,128)}, u32[]{:S(2)}) copy-start(s32[2048,1]{0,1:T(1,128)} %mul.65) | copy-start | bytes 24580
  95.1 1.8 copy-start.2
  145.0 1.8 copy-start.2
  185.2 12.9 %copy-start.7 = (f32[1024]{0:T(1024)S(1)}, f32[1024]{0:T(1024)}, u32[]{:S(2)}) copy-start(f32[1024]{0:T(1024)} %param.21) | copy-start | bytes 12292
  185.2 9.5 %all-to-all-start.3 = ((bf16[2,256,4,128]{3,2,0,1:T(4,128)(2,1)}), bf16[2,256,4,128]{3,2,0,1:T(4,128)(2,1)S(1)}, u32[]{:S(2)}, u32[]{:S(2)}) async-start(bf16[2,256,4,128]{3,2,0,1:T(4,128)(2,1)} %get-tuple-element.80), calls=%async_computation.3 | async-start | bytes 1048576 | tf_op jit(solution)/shard_map/all_to_all | solution.py:109
  232.3 11.3 %copy-start.8 = (s32[2,128]{1,0:T(2,128)S(1)}, s32[2,128]{1,0:T(2,128)}, u32[]{:S(2)}) copy-start(s32[2,128]{1,0:T(2,128)} %param.25) | copy-start | bytes 3076
  232.3 192.9 %all-to-all-start.4 = ((bf16[16,256,1024]{2,1,0:T(8,128)(2,1)}), bf16[16,256,1024]{2,1,0:T(8,128)(2,1)}, u32[]{:S(2)}, u32[]{:S(2)}) async-start(bf16[16,256,1024]{2,1,0:T(8,128)(2,1)} %bitcast.189), calls=%async_computation.4 | async-start | bytes 16777216 | tf_op jit(solution)/shard_map/all_to_all | solution.py:155
  242.9 187.3 %all-gather.2.cloned.1.call-start = ((), (), s32[]{:S(2)}) async-start(), calls=%async_computation.7 | async-start | bytes 4718592 | tf_op jit(solution)/shard_map/all_gather | solution.py:154
  425.2 32.3 %all-to-all-start.6 = ((s32[16,1,16]{2,1,0:T(1,128)}), s32[16,1,16]{2,1,0:T(1,128)S(1)}, u32[]{:S(2)}, u32[]{:S(2)}) async-start(s32[16,1,16]{2,1,0:T(1,128)} %all_to_all.81), calls=%async_computation.6 | async-start | bytes 16384 | tf_op jit(solution)/shard_map/all_to_all | solution.py:125
  457.6 0.6 copy-start.5
  458.2 315.7 %all-to-all-start.5 = ((bf16[16,256,1024]{2,1,0:T(8,128)(2,1)}), bf16[16,256,1024]{2,1,0:T(8,128)(2,1)}, u32[]{:S(2)}, u32[]{:S(2)}) async-start(bf16[16,256,1024]{2,1,0:T(8,128)(2,1)} %convolution_convert_fusion), calls=%async_computation.5 | async-start | bytes 16777216 | tf_op jit(solution)/shard_map/all_to_all | solution.py:168
  476.5 3.0 copy-start.1
  482.0 7.9 collective-permute-start
  486.3 197.4 %copy-start.3 = (bf16[1,16,4,16,128]{4,3,2,1,0:T(8,128)(2,1)S(1)}, bf16[1,16,4,16,128]{4,3,2,1,0:T(8,128)(2,1)}, u32[]{:S(2)}) copy-start(bf16[1,16,4,16,128]{4,3,2,1,0:T(8,128)(2,1)} %get-tuple-element.133) | copy-start | bytes 786436
  486.3 29.9 %collective-permute-start.1 = (bf16[1,16,4,16,128]{4,3,2,1,0:T(8,128)(2,1)}, bf16[1,16,4,16,128]{4,3,2,1,0:T(8,128)(2,1)S(1)}, u32[]{:S(2)}, u32[]{:S(2)}) collective-permute-start(bf16[1,16,4,16,128]{4,3,2,1,0:T(8,128)(2,1)} %get-tuple-element.145), channel_id=1, source_target_pairs={{0,4},{2,6},{4,0},{6,2},{8,12},{10,14},{12,8},{14,10},{16,20},{18,... | collective-permute-start | bytes 786440 | tf_op jit(solution)/shard_map/ppermute | solution.py:21
  486.7 35.4 %collective-permute-start.2 = (bf16[1,16,4,16,128]{4,3,2,1,0:T(8,128)(2,1)}, bf16[1,16,4,16,128]{4,3,2,1,0:T(8,128)(2,1)S(1)}, u32[]{:S(2)}, u32[]{:S(2)}) collective-permute-start(bf16[1,16,4,16,128]{4,3,2,1,0:T(8,128)(2,1)} %get-tuple-element.144), channel_id=1, source_target_pairs={{0,6},{2,4},{4,2},{6,0},{8,14},{10,12},{12,10},{14,8},{16,22},{18,... | collective-permute-start | bytes 786440 | tf_op jit(solution)/shard_map/ppermute | solution.py:21
  488.2 119.1 %collective-permute-start.3 = (bf16[1,16,4,16,128]{4,3,2,1,0:T(8,128)(2,1)}, bf16[1,16,4,16,128]{4,3,2,1,0:T(8,128)(2,1)S(1)}, u32[]{:S(2)}, u32[]{:S(2)}) collective-permute-start(bf16[1,16,4,16,128]{4,3,2,1,0:T(8,128)(2,1)} %get-tuple-element.143), channel_id=1, source_target_pairs={{0,8},{2,10},{4,12},{6,14},{8,0},{10,2},{12,4},{14,6},{16,24},{18,... | collective-permute-start | bytes 786440 | tf_op jit(solution)/shard_map/ppermute | solution.py:21
  488.5 125.3 %collective-permute-start.4 = (bf16[1,16,4,16,128]{4,3,2,1,0:T(8,128)(2,1)}, bf16[1,16,4,16,128]{4,3,2,1,0:T(8,128)(2,1)S(1)}, u32[]{:S(2)}, u32[]{:S(2)}) collective-permute-start(bf16[1,16,4,16,128]{4,3,2,1,0:T(8,128)(2,1)} %get-tuple-element.142), channel_id=1, source_target_pairs={{0,10},{2,8},{4,14},{6,12},{8,2},{10,0},{12,6},{14,4},{16,26},{18,... | collective-permute-start | bytes 786440 | tf_op jit(solution)/shard_map/ppermute | solution.py:21
  489.9 127.7 %collective-permute-start.5 = (bf16[1,16,4,16,128]{4,3,2,1,0:T(8,128)(2,1)}, bf16[1,16,4,16,128]{4,3,2,1,0:T(8,128)(2,1)S(1)}, u32[]{:S(2)}, u32[]{:S(2)}) collective-permute-start(bf16[1,16,4,16,128]{4,3,2,1,0:T(8,128)(2,1)} %get-tuple-element.141), channel_id=1, source_target_pairs={{0,12},{2,14},{4,8},{6,10},{8,4},{10,6},{12,0},{14,2},{16,28},{18,... | collective-permute-start | bytes 786440 | tf_op jit(solution)/shard_map/ppermute | solution.py:21
  516.3 109.4 %collective-permute-start.6 = (bf16[1,16,4,16,128]{4,3,2,1,0:T(8,128)(2,1)}, bf16[1,16,4,16,128]{4,3,2,1,0:T(8,128)(2,1)S(1)}, u32[]{:S(2)}, u32[]{:S(2)}) collective-permute-start(bf16[1,16,4,16,128]{4,3,2,1,0:T(8,128)(2,1)} %get-tuple-element.140), channel_id=1, source_target_pairs={{0,14},{2,12},{4,10},{6,8},{8,6},{10,4},{12,2},{14,0},{16,30},{18,... | collective-permute-start | bytes 786440 | tf_op jit(solution)/shard_map/ppermute | solution.py:21
  522.1 156.2 %collective-permute-start.7 = (bf16[1,16,4,16,128]{4,3,2,1,0:T(8,128)(2,1)}, bf16[1,16,4,16,128]{4,3,2,1,0:T(8,128)(2,1)S(1)}, u32[]{:S(2)}, u32[]{:S(2)}) collective-permute-start(bf16[1,16,4,16,128]{4,3,2,1,0:T(8,128)(2,1)} %get-tuple-element.139), channel_id=1, source_target_pairs={{0,16},{2,18},{4,20},{6,22},{8,24},{10,26},{12,28},{14,30},{16,0},... | collective-permute-start | bytes 786440 | tf_op jit(solution)/shard_map/ppermute | solution.py:21
  607.3 76.5 %collective-permute-start.8 = (bf16[1,16,4,16,128]{4,3,2,1,0:T(8,128)(2,1)}, bf16[1,16,4,16,128]{4,3,2,1,0:T(8,128)(2,1)S(1)}, u32[]{:S(2)}, u32[]{:S(2)}) collective-permute-start(bf16[1,16,4,16,128]{4,3,2,1,0:T(8,128)(2,1)} %get-tuple-element.138), channel_id=1, source_target_pairs={{0,18},{2,16},{4,22},{6,20},{8,26},{10,24},{12,30},{14,28},{16,2},... | collective-permute-start | bytes 786440 | tf_op jit(solution)/shard_map/ppermute | solution.py:21
  613.8 81.3 %collective-permute-start.9 = (bf16[1,16,4,16,128]{4,3,2,1,0:T(8,128)(2,1)}, bf16[1,16,4,16,128]{4,3,2,1,0:T(8,128)(2,1)S(1)}, u32[]{:S(2)}, u32[]{:S(2)}) collective-permute-start(bf16[1,16,4,16,128]{4,3,2,1,0:T(8,128)(2,1)} %get-tuple-element.137), channel_id=1, source_target_pairs={{0,20},{2,22},{4,16},{6,18},{8,28},{10,30},{12,24},{14,26},{16,4},... | collective-permute-start | bytes 786440 | tf_op jit(solution)/shard_map/ppermute | solution.py:21
  617.6 94.3 %collective-permute-start.10 = (bf16[1,16,4,16,128]{4,3,2,1,0:T(8,128)(2,1)}, bf16[1,16,4,16,128]{4,3,2,1,0:T(8,128)(2,1)S(1)}, u32[]{:S(2)}, u32[]{:S(2)}) collective-permute-start(bf16[1,16,4,16,128]{4,3,2,1,0:T(8,128)(2,1)} %get-tuple-element.136), channel_id=1, source_target_pairs={{0,22},{2,20},{4,18},{6,16},{8,30},{10,28},{12,26},{14,24},{16,6},... | collective-permute-start | bytes 786440 | tf_op jit(solution)/shard_map/ppermute | solution.py:21
  625.6 93.9 %collective-permute-start.11 = (bf16[1,16,4,16,128]{4,3,2,1,0:T(8,128)(2,1)}, bf16[1,16,4,16,128]{4,3,2,1,0:T(8,128)(2,1)S(1)}, u32[]{:S(2)}, u32[]{:S(2)}) collective-permute-start(bf16[1,16,4,16,128]{4,3,2,1,0:T(8,128)(2,1)} %get-tuple-element.135), channel_id=1, source_target_pairs={{0,24},{2,26},{4,28},{6,30},{8,16},{10,18},{12,20},{14,22},{16,8},... | collective-permute-start | bytes 786440 | tf_op jit(solution)/shard_map/ppermute | solution.py:21
  678.2 47.8 %collective-permute-start.12 = (bf16[1,16,4,16,128]{4,3,2,1,0:T(8,128)(2,1)}, bf16[1,16,4,16,128]{4,3,2,1,0:T(8,128)(2,1)S(1)}, u32[]{:S(2)}, u32[]{:S(2)}) collective-permute-start(bf16[1,16,4,16,128]{4,3,2,1,0:T(8,128)(2,1)} %get-tuple-element.134), channel_id=1, source_target_pairs={{0,26},{2,24},{4,30},{6,28},{8,18},{10,16},{12,22},{14,20},{16,10}... | collective-permute-start | bytes 786440 | tf_op jit(solution)/shard_map/ppermute | solution.py:21
  683.7 47.0 %collective-permute-start.13 = (bf16[1,16,4,16,128]{4,3,2,1,0:T(8,128)(2,1)S(1)}, bf16[1,16,4,16,128]{4,3,2,1,0:T(8,128)(2,1)S(1)}, u32[]{:S(2)}, u32[]{:S(2)}) collective-permute-start(bf16[1,16,4,16,128]{4,3,2,1,0:T(8,128)(2,1)S(1)} %copy-done.3), channel_id=1, source_target_pairs={{0,28},{2,30},{4,24},{6,26},{8,20},{10,22},{12,16},{14,18},{16,12}... | collective-permute-start | bytes 786440 | tf_op jit(solution)/shard_map/ppermute | solution.py:21
  695.1 41.4 %collective-permute-start.14 = (bf16[1,16,4,16,128]{4,3,2,1,0:T(8,128)(2,1)S(1)}, bf16[1,16,4,16,128]{4,3,2,1,0:T(8,128)(2,1)S(1)}, u32[]{:S(2)}, u32[]{:S(2)}) collective-permute-start(bf16[1,16,4,16,128]{4,3,2,1,0:T(8,128)(2,1)S(1)} %get-tuple-element.132), channel_id=1, source_target_pairs={{0,30},{2,28},{4,26},{6,24},{8,22},{10,20},{12,18},{14,16},{16,14}... | collective-permute-start | bytes 786440 | tf_op jit(solution)/shard_map/ppermute | solution.py:21
Sparse Core Ops, SparseCore 0:
  245.3 44.5 all-gather.1
